TPU v7x, 128 devices: a whole 4x4x4 slice. The times are simulated.
128 devices in a mesh: wave: 16 (over y, z_lo, core), pole: 8 (over x, z_hi).
Axes of the slice: x: 4, y: 4, z: 4 (z_hi: 2, z_lo: 2; z = z_hi * 2 + z_lo), core: 2. Of those that a mesh axis runs over, the one named last changes fastest.
Arguments:
- grid: float32 [6, 256, 3072], P(None, None, 'wave'), may hold values from -6 to 6
- legendre: bfloat16 [256, 2, 1536, 1024], P('wave', None, None, 'pole'), may hold values from -0.15625 to 0.15625
- wave_table: int32 [256], replicated, may hold values from 0 to 255, each once
- pole_table: float32 [4, 64], replicated, may hold values from -1.5 to 2.5, as said below
- pole_index: int32 [32], replicated, may hold values from 0 to 63
Outputs:
- next_state: float32 [6, 2, 256, 1024], P(None, None, 'wave', 'pole')
Inputs may be any that keep to these rules, and one draw needn't show every extreme that they name: Slot s holds zonal wavenumber wave_table[s], every wavenumber of 0 to 255 once; row s of legendre belongs to it. `pole_table`: shift real parts lie in 1.5 to 2.5, shift imaginary parts in -1.5 to 1.5, weights in -1.2 to 1.2.
All inputs are finite; a program needn't handle non-finite values.
Results may differ from a plain program's by a relative error of at most 0.0003.
Values sent between devices are 32-bit elements; how exact they have to be, the bound alone decides.
No kernel may reach another device: no remote copies, remote signals or barrier semaphores. Data moves between devices by JAX's collectives and lax.ppermute only.
A program may use at most 128 MiB of HBM per device.

v0:
```python
import jax
import jax.numpy as jnp
from jax import lax
from jax.sharding import PartitionSpec as P

SWEEPS = 8
coriolis_step = 1.2
gravity_step = 0.0008


def split_high(values):
    upper_part = values.astype(jnp.bfloat16)
    kept = lax.optimization_barrier(upper_part)
    lower_part = (values - kept.astype(jnp.float32)).astype(jnp.bfloat16)
    return (upper_part, lower_part)


def coefficients(wavenum, count):
    index = jnp.arange(count, dtype=jnp.int32).astype(jnp.float32)
    parity = jnp.arange(2, dtype=jnp.int32).astype(jnp.float32)
    order = (2.0 * index[None, :] + parity[:, None])[:, None, :]
    wave = wavenum[None, :, None]
    degree = wave + order
    product = degree * (degree + 1.0)
    rossby = coriolis_step * wave / jnp.maximum(product, 2.0)
    gravity = gravity_step * jnp.sqrt(product)
    e_lo = jnp.sqrt(order * (2.0 * wave + order) / jnp.maximum(4.0 * degree * degree - 1.0, 1.0))
    after = order + 1.0
    upper_deg = degree + 1.0
    e_hi = jnp.sqrt(
        after * (2.0 * wave + after) / jnp.maximum(4.0 * upper_deg * upper_deg - 1.0, 1.0)
    )
    return (e_lo, e_hi, rossby, gravity)


def cmul(are, aim, bre, bim):
    return (are * bre - aim * bim, are * bim + aim * bre)


def zero_extend(field):
    return jnp.pad(field, ((0, 0), (0, 0), (0, 0), (0, 0), (1, 1)))


def solve(spectra, coef, shifts, extend):
    e_lo, e_hi, rossby, gravity = coef
    count = spectra.shape[3]
    shift_re = shifts[:, 0][:, None, None, None]
    shift_im = shifts[:, 1][:, None, None, None]
    weight_re = shifts[:, 2][:, None, None, None]
    weight_im = shifts[:, 3][:, None, None, None]
    z0r, z0i = (spectra[0][None], spectra[1][None])
    d0r, d0i = (spectra[2][None], spectra[3][None])
    h0r, h0i = (spectra[4][None], spectra[5][None])
    b_re = shift_re + 0.0 * rossby[None]
    b_im = shift_im + rossby[None]
    b_mag = b_re * b_re + b_im * b_im
    inv_re, inv_im = (b_re / b_mag, -b_im / b_mag)
    det_re, det_im = cmul(b_re, b_im, shift_re, shift_im)
    det_re = det_re + gravity[None] * gravity[None]
    det_mag = det_re * det_re + det_im * det_im
    dinv_re, dinv_im = (det_re / det_mag, -det_im / det_mag)
    grav = gravity[None]
    hb_re, hb_im = cmul(b_re, b_im, h0r, h0i)
    zr, zi, dr, di, hr, hi = (z0r, z0i, d0r, d0i, h0r, h0i)
    for sweep in range(SWEEPS):
        if sweep == 0:
            rzr, rzi, rdr, rdi = (z0r, z0i, d0r, d0i)
        else:
            both = jnp.stack([zr, zi, dr, di], axis=0)
            ext = extend(both)
            lower = jnp.stack([ext[:, :, 1, :, 0:count], ext[:, :, 0, :, 1 : count + 1]], axis=2)
            upper = jnp.stack(
                [ext[:, :, 1, :, 1 : count + 1], ext[:, :, 0, :, 2 : count + 2]], axis=2
            )
            near = e_lo * lower + e_hi * upper
            rzr = z0r - coriolis_step * near[2]
            rzi = z0i - coriolis_step * near[3]
            rdr = d0r + coriolis_step * near[0]
            rdi = d0i + coriolis_step * near[1]
        zr, zi = cmul(rzr, rzi, inv_re, inv_im)
        nd_re, nd_im = cmul(shift_re, shift_im, rdr, rdi)
        nd_re = nd_re + grav * h0r
        nd_im = nd_im + grav * h0i
        nh_re = hb_re - grav * rdr
        nh_im = hb_im - grav * rdi
        dr, di = cmul(nd_re, nd_im, dinv_re, dinv_im)
        hr, hi = cmul(nh_re, nh_im, dinv_re, dinv_im)
    parts = []
    for field_re, field_im in ((zr, zi), (dr, di), (hr, hi)):
        out_re, out_im = cmul(weight_re, weight_im, field_re, field_im)
        parts.append(jnp.sum(out_re, axis=0))
        parts.append(jnp.sum(out_im, axis=0))
    return jnp.stack(parts, axis=0)


def lookup(pole_table, chosen):
    columns = jnp.arange(pole_table.shape[1], dtype=jnp.int32)
    onehot = (chosen[:, None] == columns[None, :]).astype(jnp.float32)
    return jnp.dot(onehot, jnp.transpose(pole_table), precision=lax.Precision.HIGHEST)


def shards(grid, legendre, wave_table, pole_table, pole_index):
    slots = legendre.shape[0]
    local_k = legendre.shape[3]
    lat_rows = grid.shape[2]
    wave_count = lax.axis_size("wave")
    half_count = wave_count // 2
    columns = jnp.take(grid, wave_table, axis=1)
    regrouped = lax.all_to_all(columns[None], "wave", split_axis=2, concat_axis=0, tiled=True)
    north = regrouped[:half_count]
    south = regrouped[half_count:]
    parts = jnp.stack([north + south, north - south], axis=0)
    high, low = split_high(parts)
    leg_blocks = legendre.reshape(slots, 2, half_count, lat_rows, local_k)
    first = jnp.einsum("mpwlk,pwcml->cpmk", leg_blocks, high, preferred_element_type=jnp.float32)
    second = jnp.einsum("mpwlk,pwcml->cpmk", leg_blocks, low, preferred_element_type=jnp.float32)
    spectra = first + second
    own_waves = lax.dynamic_slice_in_dim(wave_table, lax.axis_index("wave") * slots, slots).astype(
        jnp.float32
    )
    whole = lax.all_gather(spectra, "pole", axis=3, tiled=True)
    per_device = pole_index.shape[0] // lax.axis_size("pole")
    chosen = lax.dynamic_slice_in_dim(pole_index, lax.axis_index("pole") * per_device, per_device)
    coef = coefficients(own_waves, whole.shape[3])
    partial_terms = solve(whole, coef, lookup(pole_table, chosen), zero_extend)
    result = lax.psum_scatter(partial_terms, "pole", scatter_dimension=3, tiled=True)
    return result


def solution(mesh):
    in_specs = (P(None, None, "wave"), P("wave", None, None, "pole"), P(), P(), P())
    out_specs = P(None, None, "wave", "pole")
    return jax.shard_map(shards, mesh=mesh, in_specs=in_specs, out_specs=out_specs, check_vma=False)
```

profile of v0, /device:TPU:0, one launch (start us, length us, event | category | flops | bytes accessed | tf_op | source)
XLA Modules:
  0.0 192.9 jit_solution(7145403172599582811)
XLA Ops:
  6.5 0.7 compare_and_fusion
  7.2 0.7 compare_select_fusion
  7.9 2.8 %copy.19 = f32[6,256,192]{2,0,1:T(8,128)} copy(f32[6,256,192]{1,2,0:T(8,128)} %param.5) | data formatting | bytes 2359296 | tf_op args[0]
  10.8 2.3 %gather_fusion = f32[256,6,192]{2,1,0:T(8,128)S(1)} fusion(f32[6,256,192]{2,0,1:T(8,128)} %copy.19, s32[1024]{0:T(1024)S(1)} %pad_clamp_fusion), kind=kCustom, calls=%fused_computation | custom fusion | bytes 2360320 | tf_op jit(solution)/shard_map/jit(_take)/gather | solution.py:108
  13.1 0.3 bitcast_select_fusion
  13.5 2.8 %copy.20 = f32[1,6,256,192]{3,0,1,2:T(1,128)} copy(f32[1,6,256,192]{3,1,2,0:T(8,128)S(1)} %bitcast_select_fusion) | data formatting | bytes 2359296 | tf_op jit(solution)/shard_map/jit(_take)/select_n | solution.py:108
  16.2 6.1 %all-to-all-start = ((f32[1,6,256,192]{3,0,1,2:T(1,128)}), f32[1,6,256,192]{3,0,1,2:T(1,128)S(1)}, u32[]{:S(2)}, u32[]{:S(2)}) async-start(f32[1,6,256,192]{3,0,1,2:T(1,128)} %copy.20), calls=%async_computation | async-start | bytes 3145728 | tf_op jit(solution)/shard_map/all_to_all | solution.py:109
  22.4 0.0 reduce-scatter.2.cloned.1.call-start
  22.5 0.1 broadcast_multiply_fusion.2
  22.6 0.1 dynamic_slice.6
  22.7 0.2 fusion.101
  22.8 0.1 broadcast_add_fusion
  22.9 0.3 fusion.97
  23.2 21.3 %all-to-all-done = f32[1,6,256,192]{3,0,1,2:T(1,128)S(1)} async-done(((f32[1,6,256,192]{3,0,1,2:T(1,128)}), f32[1,6,256,192]{3,0,1,2:T(1,128)S(1)}, u32[]{:S(2)}, u32[]{:S(2)}) %all-to-all-start) | async-done | bytes 1179680 | tf_op jit(solution)/shard_map/all_to_all | solution.py:109
  44.5 0.1 copy.21
  44.6 0.0 slice-start
  44.7 0.9 copy.56
  45.6 0.2 add_bitcast_fusion
  45.8 0.0 slice-start.1
  45.9 0.2 fusion.11
  46.1 0.0 slice-start.2
  46.1 6.8 %fusion.12 = f32[2,16,6,128]{3,2,1,0:T(8,128)S(1)} fusion(bf16[2,8,6,16,192]{4,2,1,3,0:T(8,128)(2,1)S(1)} %fusion.11, bf16[16,2,8,192,128]{4,3,2,1,0:T(8,128)(2,1)} %bitcast.123), kind=kOutput, calls=%fused_computation.72 | convolution fusion | flops 75497472 | bytes 13271040 | tf_op jit(solution)/shard_map/mpwlk,pwcml->cpmk/dot_general | solution.py:115
  52.9 0.1 slice-done.2
  53.1 2.2 %fusion.21 = f32[6,2,16,128]{3,0,2,1:T(8,128)S(1)} fusion(f32[2,16,6,128]{3,2,1,0:T(8,128)S(1)} %fusion.12, bf16[16,2,8,192,128]{4,3,2,1,0:T(8,128)(2,1)S(1)} %bitcast.126, bf16[2,8,6,16,192]{4,2,1,3,0:T(8,128)(2,1)S(1)} %fusion.11, f32[1,8,6,16,192]{4,2,1,3,0:T(8,128)S(1)} %get-tuple-element.86, f32[1,8,6,16,192]{4,2,1,3,0:T(8,128)S(1)} %get-tuple-element.85), kind=kOutput, calls=%fused_computation.75 | convolution fusion | flops 76701696 | bytes 14548992 | tf_op jit(solution)/shard_map/mpwlk,pwcml->cpmk/dot_general | solution.py:116
  55.2 37.6 %all_gather.3 = f32[6,2,16,1024]{3,0,2,1:T(8,128)S(1)} all-gather(f32[6,2,16,128]{3,0,2,1:T(8,128)S(1)} %fusion.21), channel_id=1, replica_groups=mesh['wave'=16,'pole'=8] {'pole'}, dimensions={3}, use_global_device_ids=true | all-gather | bytes 884736 | tf_op jit(solution)/shard_map/all_gather | solution.py:121
  92.8 0.9 fusion.99
  93.7 0.1 copy_bitcast_fusion.3
  93.8 0.1 copy_bitcast_fusion.7
  93.8 0.1 copy_bitcast_fusion.5
  93.9 0.8 multiply_subtract_fusion.16
  94.7 0.2 pad_maximum_fusion.1
  95.0 0.8 fusion.110
  95.8 0.5 fusion.4
  96.3 0.9 multiply_subtract_fusion.14
  97.2 0.2 pad_maximum_fusion.2
  97.4 0.8 fusion.109
  98.3 0.5 fusion.5
  98.8 0.9 multiply_subtract_fusion.12
  99.7 0.2 pad_maximum_fusion.3
  99.9 0.8 fusion.108
  100.7 0.5 fusion.6
  101.2 0.9 multiply_subtract_fusion.10
  102.2 0.2 pad_maximum_fusion.4
  102.4 0.8 fusion.107
  103.2 0.5 fusion.7
  103.7 0.9 multiply_subtract_fusion.8
  104.6 0.2 pad_maximum_fusion.5
  104.8 1.0 fusion.106
  105.9 0.5 fusion.8
  106.4 0.9 multiply_subtract_fusion.6
  107.3 0.2 pad_maximum_fusion.6
  107.5 0.8 fusion.105
  108.3 0.5 fusion.9
  108.9 0.9 multiply_subtract_fusion.4
  109.8 0.2 pad_maximum_fusion.7
  110.0 0.8 fusion.104
  110.8 0.5 fusion.10
  111.3 0.4 multiply_subtract_fusion.2
  111.7 0.1 copy_bitcast_fusion.1
  111.8 0.7 multiply_add_fusion
  112.5 1.1 add_reduce_fusion
  113.7 0.9 copy-done.2
  114.5 0.0 reduce-scatter.2.cloned.1.call-update
  114.6 71.5 %reduce-scatter.2.cloned.1.call-done = f32[6,2,16,128]{3,2,1,0:T(8,128)} async-done(((f32[6,2,16,1024]{3,2,1,0:T(8,128)}), f32[6,2,16,128]{3,2,1,0:T(8,128)}) %reduce-scatter.2.cloned.1.call-update) | async-done | bytes 98320 | tf_op jit(solution)/shard_map/reduce_scatter | solution.py:126
  (23 shorter events, 0.1 us)
Async XLA Ops:
  6.5 16.1 %copy-start = (f32[4,64]{1,0:T(4,128)S(1)}, f32[4,64]{1,0:T(4,128)}, u32[]{:S(2)}) copy-start(f32[4,64]{1,0:T(4,128)} %param.8) | copy-start | bytes 3076
  16.2 6.2 %copy-start.3 = (s32[256]{0:T(256)S(1)}, s32[256]{0:T(256)}, u32[]{:S(2)}) copy-start(s32[256]{0:T(256)} %param.7) | copy-start | bytes 3076
  16.2 6.3 %copy-start.4 = (s32[32]{0:T(128)S(1)}, s32[32]{0:T(128)}, u32[]{:S(2)}) copy-start(s32[32]{0:T(128)} %param.9) | copy-start | bytes 388
  16.2 28.2 %all-to-all-start = ((f32[1,6,256,192]{3,0,1,2:T(1,128)}), f32[1,6,256,192]{3,0,1,2:T(1,128)S(1)}, u32[]{:S(2)}, u32[]{:S(2)}) async-start(f32[1,6,256,192]{3,0,1,2:T(1,128)} %copy.20), calls=%async_computation | async-start | bytes 3145728 | tf_op jit(solution)/shard_map/all_to_all | solution.py:109
  22.4 163.6 %reduce-scatter.2.cloned.1.call-start = ((), (), s32[]{:S(2)}) async-start(), calls=%async_computation.2 | async-start | bytes 884736 | tf_op jit(solution)/shard_map/reduce_scatter | solution.py:126
  44.6 8.3 %slice-start = ((s8[12582912]{0:T(1024)(128)(4,1)}), s8[4194304]{0:T(1024)(128)(4,1)S(1)}, s32[]{:S(2)}) async-start(s8[12582912]{0:T(1024)(128)(4,1)} %bitcast.124), calls=%async_computation.3 | async-start | bytes 8388608
  45.8 7.1 %slice-start.1 = ((s8[12582912]{0:T(1024)(128)(4,1)}), s8[4194304]{0:T(1024)(128)(4,1)S(1)}, s32[]{:S(2)}) async-start(s8[12582912]{0:T(1024)(128)(4,1)} %bitcast.124), calls=%async_computation.4 | async-start | bytes 8388608
  46.1 6.9 %slice-start.2 = ((s8[12582912]{0:T(1024)(128)(4,1)}), s8[4194304]{0:T(1024)(128)(4,1)S(1)}, s32[]{:S(2)}) async-start(s8[12582912]{0:T(1024)(128)(4,1)} %bitcast.124), calls=%async_computation.5 | async-start | bytes 8388608
  112.5 73.6 %copy-start.1 = (f32[4,64]{1,0:T(4,128)S(1)}, f32[4,64]{1,0:T(4,128)}, u32[]{:S(2)}) copy-start(f32[4,64]{1,0:T(4,128)} %param.8) | copy-start | bytes 3076
  113.7 0.9 copy-start.2
Sparse Core Ops, SparseCore 0:
  114.7 71.3 reduce-scatter.1
where the time goes:
time: 193 us
  waiting for transfers between devices  92.8 us (48%)
  blocking collectives  37.6 us (19%)
  other arithmetic  17 us (9%)
  local copies, waits for them, and re-layouts  16.4 us (8%)
  between operations  13.8 us (7%)
  matrix products  9.14 us (5%)
  starting transfers between devices  6.18 us (3%)
    reduce_scatter x1, waiting for transfers between devices, shards(): lax.psum_scatter(partial_terms, 'pole', scatter_dimension=3, tiled=True)  71.5 us
    all_gather x1, blocking collectives, shards(): whole = lax.all_gather(spectra, 'pole', axis=3, tiled=True)  37.6 us
    all_to_all x1, waiting for transfers between devices, shards(): lax.all_to_all(columns[None], 'wave', split_axis=2, concat_axis=0, tiled=...  21.3 us
    dot_general x1, matrix products, shards(): jnp.einsum('mpwlk,pwcml->cpmk', leg_blocks, high, preferred_element_type=...  6.8 us
    sub x8, other arithmetic, cmul(): return (are * bre - aim * bim, are * bim + aim * bre)  6.75 us
    all_to_all x1, starting transfers between devices, shards(): lax.all_to_all(columns[None], 'wave', split_axis=2, concat_axis=0, tiled=...  6.14 us
    slice x7, local copies, waits for them, and re-layouts, solve(): ext[:, :, 1, :, 1:count + 1]  5.96 us
    unnamed x26, local copies, waits for them, and re-layouts  4.13 us
  transfers between devices with their start and end apart: 2, of which 2 were waited for; matrix products, arithmetic and copies ran while one was open for 0% of the time, Pallas kernels for 0%

commit v1 on v0

--- a/solution.py
+++ b/solution.py
@@ -2,6 +2,7 @@
 import jax.numpy as jnp
 from jax import lax
 from jax.sharding import PartitionSpec as P
+from jax.lax import all_to_all, axis_size
 
 SWEEPS = 8
 coriolis_step = 1.2
@@ -106,7 +107,9 @@
     wave_count = lax.axis_size("wave")
     half_count = wave_count // 2
     columns = jnp.take(grid, wave_table, axis=1)
-    regrouped = lax.all_to_all(columns[None], "wave", split_axis=2, concat_axis=0, tiled=True)
+    regrouped = jnp.concatenate(
+        all_to_all(jnp.stack(jnp.split(columns[None], axis_size("wave"), 2)), "wave", 0, 0), 0
+    )
     north = regrouped[:half_count]
     south = regrouped[half_count:]
     parts = jnp.stack([north + south, north - south], axis=0)

time: 193 us -> 192 us (level)
    select_n x1 -> x0, local copies, waits for them, and re-layouts: 2.78 us -> none  [shards(): columns = jnp.take(grid, wave_table, axis=1)]
    unnamed x26 -> x41, local copies, waits for them, and re-layouts: 4.13 us -> 4.33 us
where the time goes in v1:
time: 192 us
  waiting for transfers between devices  92.8 us (48%)
  blocking collectives  37.6 us (20%)
  other arithmetic  17.7 us (9%)
  local copies, waits for them, and re-layouts  14.5 us (8%)
  between operations  13.9 us (7%)
  matrix products  9.3 us (5%)
  starting transfers between devices  6.18 us (3%)
    reduce_scatter x1, waiting for transfers between devices, shards(): lax.psum_scatter(partial_terms, 'pole', scatter_dimension=3, tiled=True)  71.5 us
    all_gather x1, blocking collectives, shards(): whole = lax.all_gather(spectra, 'pole', axis=3, tiled=True)  37.6 us
    all_to_all x1, waiting for transfers between devices, shards(): all_to_all(jnp.stack(jnp.split(columns[None], axis_size('wave'), 2)), 'wa...  21.3 us
    dot_general x1, matrix products, shards(): jnp.einsum('mpwlk,pwcml->cpmk', leg_blocks, high, preferred_element_type=...  6.97 us
    sub x8, other arithmetic, cmul(): return (are * bre - aim * bim, are * bim + aim * bre)  6.75 us
    all_to_all x1, starting transfers between devices, shards(): all_to_all(jnp.stack(jnp.split(columns[None], axis_size('wave'), 2)), 'wa...  6.14 us
    slice x7, local copies, waits for them, and re-layouts, solve(): ext[:, :, 1, :, 1:count + 1]  5.96 us
    unnamed x41, local copies, waits for them, and re-layouts  4.33 us
  transfers between devices with their start and end apart: 2, of which 2 were waited for; matrix products, arithmetic and copies ran while one was open for 0% of the time, Pallas kernels for 0%

profile of v1, /device:TPU:0, one launch (start us, length us, event | category | flops | bytes accessed | tf_op | source)
XLA Modules:
  0.0 192.0 jit_solution(8708339376040782265)
XLA Ops:
  6.5 0.7 compare_and_fusion
  7.2 0.7 compare_select_fusion
  7.9 2.8 %copy.47 = f32[6,256,192]{2,0,1:T(8,128)} copy(f32[6,256,192]{1,2,0:T(8,128)} %param.5) | data formatting | bytes 2359296 | tf_op args[0]
  10.8 2.3 %gather_fusion = f32[256,6,192]{2,1,0:T(8,128)S(1)} fusion(f32[6,256,192]{2,0,1:T(8,128)} %copy.47, s32[1024]{0:T(1024)S(1)} %pad_clamp_fusion), kind=kCustom, calls=%fused_computation | custom fusion | bytes 2360320 | tf_op jit(solution)/shard_map/jit(_take)/gather | solution.py:109
  13.1 0.3 bitcast_select_fusion
  13.8 1.7 copy.48
  15.4 6.1 %all-to-all-start = ((f32[16,1,6,16,192]{4,3,2,1,0:T(8,128)}), f32[16,1,6,16,192]{4,3,2,1,0:T(8,128)S(1)}, u32[]{:S(2)}, u32[]{:S(2)}) async-start(f32[16,1,6,16,192]{4,3,2,1,0:T(8,128)} %copy.48), calls=%async_computation | async-start | bytes 3145728 | tf_op jit(solution)/shard_map/all_to_all | solution.py:111
  21.6 0.0 reduce-scatter.2.cloned.1.call-start
  21.7 0.1 broadcast_multiply_fusion.2
  21.8 0.1 dynamic_slice.6
  21.8 0.2 fusion.119
  22.0 0.1 broadcast_add_fusion
  22.1 0.3 fusion.99
  22.4 21.3 %all-to-all-done = f32[16,1,6,16,192]{4,3,2,1,0:T(8,128)S(1)} async-done(((f32[16,1,6,16,192]{4,3,2,1,0:T(8,128)}), f32[16,1,6,16,192]{4,3,2,1,0:T(8,128)S(1)}, u32[]{:S(2)}, u32[]{:S(2)}) %all-to-all-start) | async-done | bytes 1179680 | tf_op jit(solution)/shard_map/all_to_all | solution.py:111
  43.7 0.1 fusion.129
  43.8 0.9 fusion.24
  44.7 0.0 slice-start.1
  44.7 0.2 fusion.11
  45.0 0.0 slice-start.2
  45.0 7.0 %fusion.12 = f32[2,16,6,128]{3,2,1,0:T(8,128)S(1)} fusion(bf16[2,8,6,16,192]{4,2,1,3,0:T(8,128)(2,1)S(1)} %fusion.11, bf16[16,2,8,192,128]{4,3,2,1,0:T(8,128)(2,1)} %bitcast.183), kind=kOutput, calls=%fused_computation.71 | convolution fusion | flops 75497472 | bytes 13271040 | tf_op jit(solution)/shard_map/mpwlk,pwcml->cpmk/dot_general | solution.py:118
  52.0 0.0 slice-done.1
  52.0 0.1 slice-done.2
  52.1 2.2 %fusion.21 = f32[6,2,16,128]{3,0,2,1:T(8,128)S(1)} fusion(f32[2,16,6,128]{3,2,1,0:T(8,128)S(1)} %fusion.12, bf16[16,2,8,192,128]{4,3,2,1,0:T(8,128)(2,1)S(1)} %bitcast.186, bf16[2,8,6,16,192]{4,2,1,3,0:T(8,128)(2,1)S(1)} %fusion.11, f32[1,8,6,16,192]{4,2,1,3,0:T(8,128)S(1)} %get-tuple-element.86, f32[1,8,6,16,192]{4,2,1,3,0:T(8,128)S(1)} %get-tuple-element.85), kind=kOutput, calls=%fused_computation.74 | convolution fusion | flops 76701696 | bytes 14548992 | tf_op jit(solution)/shard_map/mpwlk,pwcml->cpmk/dot_general | solution.py:119
  54.3 37.6 %all_gather.3 = f32[6,2,16,1024]{3,0,2,1:T(8,128)S(1)} all-gather(f32[6,2,16,128]{3,0,2,1:T(8,128)S(1)} %fusion.21), channel_id=1, replica_groups=mesh['wave'=16,'pole'=8] {'pole'}, dimensions={3}, use_global_device_ids=true | all-gather | bytes 884736 | tf_op jit(solution)/shard_map/all_gather | solution.py:124
  91.8 0.9 fusion.117
  92.8 0.1 copy_bitcast_fusion.2
  92.9 0.1 copy_bitcast_fusion.6
  92.9 0.1 copy_bitcast_fusion.4
  93.0 0.8 multiply_subtract_fusion.16
  93.8 0.2 pad_maximum_fusion.1
  94.0 0.8 fusion.128
  94.9 0.5 fusion.4
  95.4 0.9 multiply_subtract_fusion.14
  96.3 0.2 pad_maximum_fusion.2
  96.5 0.8 fusion.127
  97.3 0.5 fusion.5
  97.9 0.9 multiply_subtract_fusion.12
  98.8 0.2 pad_maximum_fusion.3
  99.0 0.8 fusion.126
  99.8 0.5 fusion.6
  100.4 0.9 multiply_subtract_fusion.10
  101.3 0.2 pad_maximum_fusion.4
  101.5 0.8 fusion.125
  102.3 0.5 fusion.7
  102.8 0.9 multiply_subtract_fusion.8
  103.8 0.2 pad_maximum_fusion.5
  104.0 1.0 fusion.124
  105.0 0.5 fusion.8
  105.5 0.9 multiply_subtract_fusion.6
  106.4 0.2 pad_maximum_fusion.6
  106.6 0.8 fusion.123
  107.5 0.5 fusion.9
  108.0 0.9 multiply_subtract_fusion.4
  108.9 0.2 pad_maximum_fusion.7
  109.1 0.8 fusion.122
  109.9 0.5 fusion.10
  110.5 0.4 multiply_subtract_fusion.2
  110.9 0.1 copy_bitcast_fusion
  110.9 0.7 multiply_add_fusion
  111.6 0.0 copy-start.1
  111.6 1.1 add_reduce_fusion
  112.8 0.9 copy-done.2
  113.7 0.0 reduce-scatter.2.cloned.1.call-update
  113.7 71.5 %reduce-scatter.2.cloned.1.call-done = f32[6,2,16,128]{3,2,1,0:T(8,128)} async-done(((f32[6,2,16,1024]{3,2,1,0:T(8,128)}), f32[6,2,16,128]{3,2,1,0:T(8,128)}) %reduce-scatter.2.cloned.1.call-update) | async-done | bytes 98320 | tf_op jit(solution)/shard_map/reduce_scatter | solution.py:129
  (38 shorter events, 0.3 us)
Async XLA Ops:
  6.5 15.3 %copy-start = (f32[4,64]{1,0:T(4,128)S(1)}, f32[4,64]{1,0:T(4,128)}, u32[]{:S(2)}) copy-start(f32[4,64]{1,0:T(4,128)} %param.8) | copy-start | bytes 3076
  15.4 6.2 %copy-start.3 = (s32[256]{0:T(256)S(1)}, s32[256]{0:T(256)}, u32[]{:S(2)}) copy-start(s32[256]{0:T(256)} %param.7) | copy-start | bytes 3076
  15.4 6.3 %copy-start.4 = (s32[32]{0:T(128)S(1)}, s32[32]{0:T(128)}, u32[]{:S(2)}) copy-start(s32[32]{0:T(128)} %param.9) | copy-start | bytes 388
  15.4 28.2 %all-to-all-start = ((f32[16,1,6,16,192]{4,3,2,1,0:T(8,128)}), f32[16,1,6,16,192]{4,3,2,1,0:T(8,128)S(1)}, u32[]{:S(2)}, u32[]{:S(2)}) async-start(f32[16,1,6,16,192]{4,3,2,1,0:T(8,128)} %copy.48), calls=%async_computation | async-start | bytes 3145728 | tf_op jit(solution)/shard_map/all_to_all | solution.py:111
  21.6 163.6 %reduce-scatter.2.cloned.1.call-start = ((), (), s32[]{:S(2)}) async-start(), calls=%async_computation.2 | async-start | bytes 884736 | tf_op jit(solution)/shard_map/reduce_scatter | solution.py:129
  43.7 8.3 %slice-start = ((s8[12582912]{0:T(1024)(128)(4,1)}), s8[4194304]{0:T(1024)(128)(4,1)S(1)}, s32[]{:S(2)}) async-start(s8[12582912]{0:T(1024)(128)(4,1)} %bitcast.184), calls=%async_computation.3 | async-start | bytes 8388608
  44.7 7.3 %slice-start.1 = ((s8[12582912]{0:T(1024)(128)(4,1)}), s8[4194304]{0:T(1024)(128)(4,1)S(1)}, s32[]{:S(2)}) async-start(s8[12582912]{0:T(1024)(128)(4,1)} %bitcast.184), calls=%async_computation.4 | async-start | bytes 8388608
  45.0 7.1 %slice-start.2 = ((s8[12582912]{0:T(1024)(128)(4,1)}), s8[4194304]{0:T(1024)(128)(4,1)S(1)}, s32[]{:S(2)}) async-start(s8[12582912]{0:T(1024)(128)(4,1)} %bitcast.184), calls=%async_computation.5 | async-start | bytes 8388608
  111.6 73.6 %copy-start.1 = (f32[4,64]{1,0:T(4,128)S(1)}, f32[4,64]{1,0:T(4,128)}, u32[]{:S(2)}) copy-start(f32[4,64]{1,0:T(4,128)} %param.8) | copy-start | bytes 3076
  112.8 0.9 copy-start.2
Sparse Core Ops, SparseCore 0:
  113.8 71.3 reduce-scatter.1
